TPU v7x, 32 devices: a whole 2x2x4 slice. The times are simulated.
32 devices in a mesh: member: 4 (over y, core), band: 8 (over z, x).
Axes of the slice: x: 2, y: 2, z: 4, core: 2. Of those that a mesh axis runs over, the one named last changes fastest.
Arguments:
- obs_values: bfloat16 [65536, 128], P(('member', 'band')), parts along dimension 0, may hold values from -6 to 6
- obs_band: int32 [65536, 1], P(('member', 'band')), parts along dimension 0, may hold values from 0 to 7; in each aligned block of 2048 rows (0 to 2047, 2048 to 4095, ...) at most 256 rows name the same one
- obs_cell: int32 [65536], P(('member', 'band')), parts along dimension 0, may hold values from 0 to 2047
- obs_offset: int32 [65536], P(('member', 'band')), parts along dimension 0, may hold values from 0 to 7
- sat_values: bfloat16 [65536, 128], P(('member', 'band')), parts along dimension 0, may hold values from -6 to 6
- sat_cell: int32 [65536], P(('member', 'band')), parts along dimension 0, may hold values from 0 to 2047
- sat_offset: int32 [65536], P(('member', 'band')), parts along dimension 0, may hold values from 0 to 7
- density_embed: float32 [128], replicated, may hold values from -3 to 3
- conv1_weight: bfloat16 [3, 3, 128, 128], replicated, may hold values from -0.1875 to 0.1875
- conv1_bias: float32 [128], replicated, may hold values from -3 to 3
- conv2_weight: bfloat16 [3, 3, 128, 256], replicated, may hold values from -0.1875 to 0.1875
- conv2_bias: float32 [256], replicated, may hold values from -3 to 3
- proj_weight: bfloat16 [256, 256], replicated, may hold values from -0.375 to 0.375
Outputs:
- latents: bfloat16 [64, 64, 256], P('member'), parts along dimension 0
There are 4 independent parts, one for each index of `member`. A program takes and returns all parts, laid end to end along the dimension named above; an argument that names none is the same for every part. Nothing has to cross between parts.
Inputs may be any that keep to these rules, and one draw needn't show every extreme that they name: `obs_band`: among the station rows of one device, at most 256 name the same band, and in every draw some band is named by exactly 256 rows of some device.
All inputs are finite; a program needn't handle non-finite values.
Results may differ from a plain program's by a relative error of at most 0.0061.
Values may be sent and summed in bfloat16 or wider, within the bound.
No kernel may reach another device: no remote copies, remote signals or barrier semaphores. Data moves between devices by JAX's collectives and lax.ppermute only.
A program may use at most 64 MiB of HBM per device.

v0:
```python
import jax
import jax.numpy as jnp
from jax import lax
from jax.sharding import PartitionSpec as P

LAT_DEV = 8
LON = 256
META = 16


def passed_along(value, axis, by):
    length = lax.axis_size(axis)
    pairs = [(i, i + by) for i in range(length) if 0 <= i + by < length]
    return lax.ppermute(value, axis, pairs)


def weights_of(offsets):
    return jnp.exp(-offsets.astype(jnp.float32) ** 2 / 32.0).astype(jnp.bfloat16)


def deposit(values, cells, weight, total_cells):
    block = min(512, total_cells)
    count = total_cells // block

    def one_block(start):
        ids = start + jnp.arange(block, dtype=jnp.int32)
        table = jnp.where(
            ids[:, None] == cells[None, :], weight[None, :], jnp.zeros((), jnp.bfloat16)
        )
        sums = jnp.dot(table, values, preferred_element_type=jnp.float32)
        density = jnp.sum(table, axis=1, dtype=jnp.float32)
        return (sums, density)

    starts = jnp.arange(count, dtype=jnp.int32) * block
    sums, density = lax.map(one_block, starts)
    return (sums.reshape(total_cells, values.shape[1]), density.reshape(total_cells))


def strided(padded, weight, bias):
    count, width, chans = padded.shape
    grid = jnp.pad(padded, ((0, 1), (1, 1), (0, 0)))
    parted = grid.reshape((count + 1) // 2, 2, (width + 2) // 2, 2, chans)
    rows = (count - 1) // 2
    cols = width // 2
    total = jnp.zeros((rows * cols, weight.shape[3]), jnp.float32)
    for first in range(3):
        for second in range(3):
            piece = parted[
                first // 2 : first // 2 + rows,
                first % 2,
                second // 2 : second // 2 + cols,
                second % 2,
                :,
            ]
            total = total + jnp.dot(
                piece.reshape(rows * cols, chans),
                weight[first, second],
                preferred_element_type=jnp.float32,
            )
    return jax.nn.gelu(total + bias, approximate=False).reshape(rows, cols, weight.shape[3])


def project(latent, proj_weight):
    flat = jnp.dot(
        latent.reshape(-1, latent.shape[2]), proj_weight, preferred_element_type=jnp.float32
    )
    return flat.astype(jnp.bfloat16).reshape(latent.shape)


def route(obs_values, obs_band, obs_cell, obs_offset, bands):
    obs_rows, d_in = obs_values.shape
    capacity = obs_rows // 8
    slots = bands * capacity
    target = obs_band[:, 0]
    choose = (target[:, None] == jnp.arange(bands, dtype=jnp.int32)[None, :]).astype(jnp.bfloat16)
    earlier = (
        jnp.arange(obs_rows, dtype=jnp.int32)[:, None]
        > jnp.arange(obs_rows, dtype=jnp.int32)[None, :]
    ).astype(jnp.bfloat16)
    before = jnp.dot(earlier, choose, preferred_element_type=jnp.float32)
    rank = jnp.sum(before * choose.astype(jnp.float32), axis=1).astype(jnp.int32)
    position = target * capacity + rank
    table = (jnp.arange(slots, dtype=jnp.int32)[:, None] == position[None, :]).astype(jnp.bfloat16)
    sent = jnp.dot(table, obs_values, preferred_element_type=jnp.float32).astype(jnp.bfloat16)
    meta = jnp.stack([obs_cell // 64, obs_cell % 64, obs_offset + 1], axis=0).astype(jnp.bfloat16)
    meta_sent = jnp.dot(meta, table.T, preferred_element_type=jnp.float32).astype(jnp.bfloat16)
    meta_sent = meta_sent.reshape(3, bands, capacity).transpose(1, 0, 2)
    meta_sent = meta_sent.reshape(bands, 3 * capacity // d_in, d_in)
    pad = jnp.zeros((bands, META - 3 * capacity // d_in, d_in), jnp.bfloat16)
    packet = jnp.concatenate([sent.reshape(bands, capacity, d_in), meta_sent, pad], axis=1)
    got = lax.all_to_all(packet, "band", split_axis=0, concat_axis=0, tiled=True)
    got_values = got[:, :capacity, :].reshape(slots, d_in)
    got_meta = got[:, capacity : capacity + 3 * capacity // d_in, :]
    got_meta = got_meta.reshape(bands, 3, capacity).transpose(1, 0, 2).reshape(3, slots)
    got_meta = got_meta.astype(jnp.int32)
    cells = got_meta[0] * 64 + got_meta[1]
    weight = jnp.where(got_meta[2] > 0, weights_of(got_meta[2] - 1), jnp.zeros((), jnp.bfloat16))
    return (got_values, cells, weight)


def body(
    obs_values,
    obs_band,
    obs_cell,
    obs_offset,
    sat_values,
    sat_cell,
    sat_offset,
    density_embed,
    conv1_weight,
    conv1_bias,
    conv2_weight,
    conv2_bias,
    proj_weight,
):
    bands = lax.axis_size("band")
    position_index = lax.axis_index("band")
    d_in = obs_values.shape[1]
    band_cells = LAT_DEV * LON
    got_values, got_cells, got_weight = route(obs_values, obs_band, obs_cell, obs_offset, bands)
    sat_sums, sat_density = deposit(sat_values, sat_cell, weights_of(sat_offset), band_cells)
    sta_sums, sta_density = deposit(got_values, got_cells, got_weight, band_cells)
    sums = sat_sums + sta_sums
    density = sat_density + sta_density
    grid0 = sums / jnp.maximum(density, 1.0)[:, None] + density[:, None] * density_embed[None, :]
    grid0 = grid0.astype(jnp.bfloat16).reshape(LAT_DEV, LON, d_in)
    above = passed_along(grid0[-3:], "band", 1)
    hidden1 = strided(jnp.concatenate([above, grid0], axis=0), conv1_weight, conv1_bias)
    keep_rows = (jnp.arange(hidden1.shape[0]) > 0) | (position_index > 0)
    hidden1 = jnp.where(keep_rows[:, None, None], hidden1, 0.0).astype(jnp.bfloat16)
    latent = strided(hidden1, conv2_weight, conv2_bias).astype(jnp.bfloat16)
    mine = project(latent, proj_weight)
    full = jnp.zeros((bands,) + mine.shape, mine.dtype)
    full = lax.dynamic_update_slice(full, mine[None], (position_index, 0, 0, 0))
    gathered = lax.psum(full, "band")
    return gathered.reshape((bands * mine.shape[0],) + mine.shape[1:])


def solution(mesh):
    placed = (
        P(("member", "band"), None),
        P(("member", "band"), None),
        P(("member", "band")),
        P(("member", "band")),
        P(("member", "band"), None),
        P(("member", "band")),
        P(("member", "band")),
        P(),
        P(),
        P(),
        P(),
        P(),
        P(),
    )
    return jax.shard_map(
        body, mesh=mesh, in_specs=placed, out_specs=P("member", None, None), check_vma=False
    )
```

profile of v0, /device:TPU:0, one launch (start us, length us, event | category | flops | bytes accessed | tf_op | source)
XLA Modules:
  0.0 151.4 jit_solution(4917465896632138708)
XLA Ops:
  6.5 2.2 %fusion.30 = f32[2048]{0:T(1024)S(1)} fusion(s32[2048]{0:T(1024)} %bitcast.178), kind=kOutput, calls=%fused_computation.58 | convolution fusion | flops 71399424 | bytes 16384 | tf_op jit(solution)/shard_map/dot_general | solution.py:80
  8.9 2.9 %fusion.23 = bf16[3,2048]{1,0:T(4,128)(2,1)S(1)} fusion(s32[2048]{0:T(1024)S(1)} %convert_add_fusion, bf16[1,2048]{1,0:T(2,128)(2,1)S(1)} %stack.18, bf16[1,2048]{1,0:T(2,128)(2,1)S(1)} %stack.17, bf16[1,2048]{1,0:T(2,128)(2,1)S(1)} %stack.16), kind=kOutput, calls=%fused_computation.33 | convolution fusion | flops 29403136 | bytes 32768 | tf_op jit(solution)/shard_map/dot_general | solution.py:86
  11.8 3.0 %fusion.21 = bf16[2048,128]{1,0:T(8,128)(2,1)S(1)} fusion(bf16[2048,128]{1,0:T(8,128)(2,1)S(1)} %copy-done, s32[2048]{0:T(1024)S(1)} %convert_add_fusion), kind=kOutput, calls=%fused_computation.31 | convolution fusion | flops 1078198272 | bytes 1056768 | tf_op jit(solution)/shard_map/dot_general | solution.py:84
  14.9 1.0 maximum_maximum_fusion
  15.9 7.4 %all-to-all-start = ((bf16[8,272,128]{2,1,0:T(8,128)(2,1)}), bf16[8,272,128]{2,1,0:T(8,128)(2,1)S(1)}, u32[]{:S(2)}, u32[]{:S(2)}) async-start(bf16[8,272,128]{2,1,0:T(8,128)(2,1)} %maximum_maximum_fusion), calls=%async_computation | async-start | bytes 1114112 | tf_op jit(solution)/shard_map/all_to_all | solution.py:91
  23.5 10.4 %while.24 = (s32[]{:T(128)}, f32[4,512,128]{2,1,0:T(8,128)S(1)}, f32[4,512]{1,0:T(4,128)S(1)}, s32[4]{0:T(128)S(1)}, s32[2048]{0:T(1024)S(1)}, /*index=5*/bf16[2...) while((s32[]{:T(128)}, f32[4,512,128]{2,1,0:T(8,128)S(1)}, ...), condition=%wide.region_2.3_spmd, body=%wide.region_0.2_spmd.sunk | while | flops 274726912 | bytes 823413 | solution.py:35
  23.5 0.6 dynamic_slice.9
  24.1 0.6 iota_add_fusion.4
  24.7 0.8 fusion.198
  25.5 0.5 convert_reduce_fusion.4
  26.1 0.6 dynamic_slice.9
  26.7 0.6 iota_add_fusion.4
  27.3 0.8 fusion.198
  28.1 0.5 convert_reduce_fusion.4
  28.7 0.6 dynamic_slice.9
  29.3 0.6 iota_add_fusion.4
  29.9 0.8 fusion.198
  30.7 0.5 convert_reduce_fusion.4
  31.3 0.6 dynamic_slice.9
  31.9 0.6 iota_add_fusion.4
  32.5 0.8 fusion.198
  33.3 0.5 convert_reduce_fusion.4
  33.9 4.6 %all-to-all-done = bf16[8,272,128]{2,1,0:T(8,128)(2,1)S(1)} async-done(((bf16[8,272,128]{2,1,0:T(8,128)(2,1)}), bf16[8,272,128]{2,1,0:T(8,128)(2,1)S(1)}, u32[]{:S(2)}, u32[]{:S(2)}) %all-to-all-start) | async-done | bytes 557088 | tf_op jit(solution)/shard_map/all_to_all | solution.py:91
  38.8 10.5 %while.25 = (s32[]{:T(128)}, f32[4,512,128]{2,1,0:T(8,128)S(1)}, f32[4,512]{1,0:T(4,128)S(1)}, s32[4]{0:T(128)S(1)}, s32[2048]{0:T(1024)S(1)}, /*index=5*/bf16[2...) while((s32[]{:T(128)}, f32[4,512,128]{2,1,0:T(8,128)S(1)}, ...), condition=%wide.region_6.7_spmd, body=%wide.region_4.6_spmd.sunk | while | flops 274726912 | bytes 823413 | solution.py:35
  38.8 0.6 dynamic_slice.10
  39.4 0.6 iota_add_fusion.5
  40.0 0.8 fusion.200
  40.8 0.5 convert_reduce_fusion.5
  41.4 0.6 dynamic_slice.10
  42.0 0.6 iota_add_fusion.5
  42.7 0.8 fusion.200
  43.4 0.5 convert_reduce_fusion.5
  44.0 0.6 dynamic_slice.10
  44.7 0.6 iota_add_fusion.5
  45.3 0.8 fusion.200
  46.7 0.6 dynamic_slice.10
  47.3 0.6 iota_add_fusion.5
  47.9 0.8 fusion.200
  50.3 3.6 %collective-permute-start = (bf16[3,256,128]{2,1,0:T(8,128)(2,1)S(1)}, bf16[3,256,128]{2,1,0:T(8,128)(2,1)S(1)}, u32[]{:S(2)}, u32[]{:S(2)}) collective-permute-start(bf16[3,256,128]{2,1,0:T(8,128)(2,1)S(1)} %bitcast.157), channel_id=1, source_target_pairs={{0,1},{1,2},{2,3},{3,4},{4,5},{5,6},{6,7},{8,9},{9,10},{10,11},{11... | collective-permute-start | bytes 589832 | tf_op jit(solution)/shard_map/ppermute | solution.py:14
  53.9 0.7 add_convert_fusion
  54.6 2.5 %collective-permute-done = bf16[3,256,128]{2,1,0:T(8,128)(2,1)S(1)} collective-permute-done((bf16[3,256,128]{2,1,0:T(8,128)(2,1)S(1)}, bf16[3,256,128]{2,1,0:T(8,128)(2,1)S(1)}, u32[]{:S(2)}, u32[]{:S(2)}) %collective-permute-start) | collective-permute-done | bytes 196640 | tf_op jit(solution)/shard_map/ppermute | solution.py:14
  57.6 3.2 %fusion.169 = (bf16[5,1,128,1,128]{4,3,2,1,0:T(2,128)(2,1)S(1)}, bf16[5,1,128,1,128]{4,3,2,1,0:T(2,128)(2,1)S(1)}, bf16[5,1,128,1,128]{4,3,2,1,0:T(2,128)(2,1)S(...) fusion(bf16[6,2,129,2,128]{4,3,2,1,0:T(2,128)(2,1)S(1)} %reshap, ...), kind=kLoop, calls=%fused_computation.236 | loop fusion | bytes 2949120 | tf_op jit(solution)/shard_map/slice | solution.py:48
  61.1 0.8 copy-done.3
  63.7 0.9 fusion.37
  67.3 0.6 convolution_convert_fusion
  67.9 0.8 copy-done.1
  68.7 74.0 %all-reduce.4.cloned.1.call-done = bf16[16,64,256]{2,1,0:T(8,128)(2,1)} async-done(((bf16[16,64,256]{2,1,0:T(8,128)(2,1)}), bf16[16,64,256]{2,1,0:T(8,128)(2,1)}) %all-reduce.4.cloned.1.call-update) | async-done | bytes 524304 | tf_op jit(solution)/shard_map/psum | solution.py:135
  142.7 1.9 %copy.62 = bf16[16,64,256]{2,1,0:T(8,128)(2,1)} copy(bf16[16,64,256]{2,1,0:T(8,128)(2,1)} %all-reduce.4.cloned.1.call-done) | data formatting | bytes 1048576
  (111 shorter events, 8.0 us)
Async XLA Ops:
  6.5 5.3 %copy-start = (bf16[2048,128]{1,0:T(8,128)(2,1)S(1)}, bf16[2048,128]{1,0:T(8,128)(2,1)}, u32[]{:S(2)}) copy-start(bf16[2048,128]{1,0:T(8,128)(2,1)} %param.17) | copy-start | bytes 1572868
  6.5 2.2 %copy-start.5 = (s32[2048,1]{0,1:T(1,128)S(1)}, s32[2048,1]{0,1:T(1,128)}, u32[]{:S(2)}) copy-start(s32[2048,1]{0,1:T(1,128)} %param.18) | copy-start | bytes 24580
  6.5 2.3 %copy-start.8 = (s32[2048]{0:T(1024)S(1)}, s32[2048]{0:T(1024)}, u32[]{:S(2)}) copy-start(s32[2048]{0:T(1024)} %param.19) | copy-start | bytes 24580
  6.5 2.3 %copy-start.6 = (s32[2048]{0:T(1024)S(1)}, s32[2048]{0:T(1024)}, u32[]{:S(2)}) copy-start(s32[2048]{0:T(1024)} %param.20) | copy-start | bytes 24580
  14.9 8.5 %copy-start.7 = (s32[2048]{0:T(1024)S(1)}, s32[2048]{0:T(1024)}, u32[]{:S(2)}) copy-start(s32[2048]{0:T(1024)} %param.23) | copy-start | bytes 24580
  15.9 7.6 %copy-start.4 = (s32[2048]{0:T(1024)S(1)}, s32[2048]{0:T(1024)}, u32[]{:S(2)}) copy-start(s32[2048]{0:T(1024)} %param.22) | copy-start | bytes 24580
  15.9 7.6 %copy-start.10 = (bf16[2048,128]{1,0:T(8,128)(2,1)S(1)}, bf16[2048,128]{1,0:T(8,128)(2,1)}, u32[]{:S(2)}) copy-start(bf16[2048,128]{1,0:T(8,128)(2,1)} %param.21) | copy-start | bytes 1572868
  15.9 22.6 %all-to-all-start = ((bf16[8,272,128]{2,1,0:T(8,128)(2,1)}), bf16[8,272,128]{2,1,0:T(8,128)(2,1)S(1)}, u32[]{:S(2)}, u32[]{:S(2)}) async-start(bf16[8,272,128]{2,1,0:T(8,128)(2,1)} %maximum_maximum_fusion), calls=%async_computation | async-start | bytes 1114112 | tf_op jit(solution)/shard_map/all_to_all | solution.py:91
  23.3 119.4 %all-reduce.4.cloned.1.call-start = ((), (), s32[]{:S(2)}) async-start(), calls=%async_computation.1 | async-start | bytes 1048576 | tf_op jit(solution)/shard_map/psum | solution.py:135
  49.4 0.7 copy-start.9
  50.3 6.8 %collective-permute-start = (bf16[3,256,128]{2,1,0:T(8,128)(2,1)S(1)}, bf16[3,256,128]{2,1,0:T(8,128)(2,1)S(1)}, u32[]{:S(2)}, u32[]{:S(2)}) collective-permute-start(bf16[3,256,128]{2,1,0:T(8,128)(2,1)S(1)} %bitcast.157), channel_id=1, source_target_pairs={{0,1},{1,2},{2,3},{3,4},{4,5},{5,6},{6,7},{8,9},{9,10},{10,11},{11... | collective-permute-start | bytes 589832 | tf_op jit(solution)/shard_map/ppermute | solution.py:14
  60.9 1.0 copy-start.3
  63.0 0.7 copy-start.13
  64.9 1.1 copy-start.2
  66.3 0.9 copy-start.11
  66.3 0.9 copy-start.12
  67.9 0.8 copy-start.1
Sparse Core Ops, SparseCore 0:
  68.8 73.8 all-reduce.3
where the time goes:
time: 152 us; the launch traced here: 151 us
  waiting for transfers between devices  81 us (53%)
  matrix products  18.2 us (12%)
  local copies, waits for them, and re-layouts  14.9 us (10%)
  between operations  14.1 us (9%)
  other arithmetic  11.9 us (8%)
  starting transfers between devices  11 us (7%)
    psum x1, waiting for transfers between devices, body(): gathered = lax.psum(full, 'band')  74 us
    all_to_all x1, starting transfers between devices, route(): lax.all_to_all(packet, 'band', split_axis=0, concat_axis=0, tiled=True)  7.41 us
    dot_general x8, matrix products, one_block(): sums = jnp.dot(table, values, preferred_element_type=jnp.float32)  6.09 us
    unnamed x49, local copies, waits for them, and re-layouts  5.18 us
    add x8, other arithmetic, one_block(): ids = start + jnp.arange(block, dtype=jnp.int32)  5.01 us
    dynamic_slice x8, local copies, waits for them, and re-layouts, deposit(): sums, density = lax.map(one_block, starts)  4.82 us
    all_to_all x1, waiting for transfers between devices, route(): lax.all_to_all(packet, 'band', split_axis=0, concat_axis=0, tiled=True)  4.57 us
    reduce_sum x8, other arithmetic, one_block(): density = jnp.sum(table, axis=1, dtype=jnp.float32)  4.39 us
  transfers between devices with their start and end apart: 3, of which 3 were waited for; matrix products, arithmetic and copies ran while one was open for 7% of the time, Pallas kernels for 0%

commit v1 on v0

--- a/solution.py
+++ b/solution.py
@@ -132,7 +132,7 @@
     mine = project(latent, proj_weight)
     full = jnp.zeros((bands,) + mine.shape, mine.dtype)
     full = lax.dynamic_update_slice(full, mine[None], (position_index, 0, 0, 0))
-    gathered = lax.psum(full, "band")
+    gathered = jnp.sum(lax.all_gather(full, "band"), axis=0)
     return gathered.reshape((bands * mine.shape[0],) + mine.shape[1:])
 
 

time: 152 us -> 154 us (1.013)
  other arithmetic: 11.9 us -> 16.5 us
  local copies, waits for them, and re-layouts: 14.9 us -> 12.3 us
    psum x1 -> x0, waiting for transfers between devices: 74 us -> none  [body(): gathered = lax.psum(full, 'band')]
    all_gather x0 -> x1, waiting for transfers between devices: none -> 73.9 us  [body(): gathered = jnp.sum(lax.all_gather(full, 'band'), axis=0)]
    reduce_sum x0 -> x1, other arithmetic: none -> 3.85 us  [body(): gathered = jnp.sum(lax.all_gather(full, 'band'), axis=0)]
    unnamed x49 -> x46, local copies, waits for them, and re-layouts: 5.18 us -> 2.4 us
where the time goes in v1:
time: 154 us; the launch traced here: 153 us
  waiting for transfers between devices  80.9 us (53%)
  matrix products  18.2 us (12%)
  other arithmetic  16.5 us (11%)
  between operations  14.1 us (9%)
  local copies, waits for them, and re-layouts  12.3 us (8%)
  starting transfers between devices  10.9 us (7%)
    all_gather x1, waiting for transfers between devices, body(): gathered = jnp.sum(lax.all_gather(full, 'band'), axis=0)  73.9 us
    all_to_all x1, starting transfers between devices, route(): lax.all_to_all(packet, 'band', split_axis=0, concat_axis=0, tiled=True)  7.29 us
    dot_general x8, matrix products, one_block(): sums = jnp.dot(table, values, preferred_element_type=jnp.float32)  6.09 us
    dynamic_slice x8, local copies, waits for them, and re-layouts, deposit(): sums, density = lax.map(one_block, starts)  5.03 us
    add x8, other arithmetic, one_block(): ids = start + jnp.arange(block, dtype=jnp.int32)  5.03 us
    all_to_all x1, waiting for transfers between devices, route(): lax.all_to_all(packet, 'band', split_axis=0, concat_axis=0, tiled=True)  4.41 us
    reduce_sum x8, other arithmetic, one_block(): density = jnp.sum(table, axis=1, dtype=jnp.float32)  4.39 us
    reduce_sum x1, other arithmetic, body(): gathered = jnp.sum(lax.all_gather(full, 'band'), axis=0)  3.85 us
  transfers between devices with their start and end apart: 3, of which 3 were waited for; matrix products, arithmetic and copies ran while one was open for 7% of the time, Pallas kernels for 0%

profile of v1, /device:TPU:0, one launch (start us, length us, event | category | flops | bytes accessed | tf_op | source)
XLA Modules:
  0.0 153.2 jit_solution(16907703933702470307)
XLA Ops:
  6.5 0.8 add_convert_fusion.1
  7.3 2.2 %fusion.30 = f32[2048]{0:T(1024)S(1)} fusion(s32[2048]{0:T(1024)} %bitcast.177), kind=kOutput, calls=%fused_computation.58 | convolution fusion | flops 71399424 | bytes 16384 | tf_op jit(solution)/shard_map/dot_general | solution.py:80
  9.6 2.9 %fusion.23 = bf16[3,2048]{1,0:T(4,128)(2,1)S(1)} fusion(s32[2048]{0:T(1024)S(1)} %convert_add_fusion, bf16[1,2048]{1,0:T(2,128)(2,1)S(1)} %stack.18, bf16[1,2048]{1,0:T(2,128)(2,1)S(1)} %stack.17, bf16[1,2048]{1,0:T(2,128)(2,1)S(1)} %stack.16), kind=kOutput, calls=%fused_computation.33 | convolution fusion | flops 29403136 | bytes 32768 | tf_op jit(solution)/shard_map/dot_general | solution.py:86
  12.6 3.0 %fusion.21 = bf16[2048,128]{1,0:T(8,128)(2,1)S(1)} fusion(bf16[2048,128]{1,0:T(8,128)(2,1)S(1)} %copy-done, s32[2048]{0:T(1024)S(1)} %convert_add_fusion), kind=kOutput, calls=%fused_computation.31 | convolution fusion | flops 1078198272 | bytes 1056768 | tf_op jit(solution)/shard_map/dot_general | solution.py:84
  15.7 1.0 maximum_maximum_fusion
  16.7 7.3 %all-to-all-start = ((bf16[8,272,128]{2,1,0:T(8,128)(2,1)}), bf16[8,272,128]{2,1,0:T(8,128)(2,1)S(1)}, u32[]{:S(2)}, u32[]{:S(2)}) async-start(bf16[8,272,128]{2,1,0:T(8,128)(2,1)} %maximum_maximum_fusion), calls=%async_computation | async-start | bytes 1114112 | tf_op jit(solution)/shard_map/all_to_all | solution.py:91
  24.1 10.6 %while.24 = (s32[]{:T(128)}, f32[4,512,128]{2,1,0:T(8,128)S(1)}, f32[4,512]{1,0:T(4,128)S(1)}, s32[4]{0:T(128)S(1)}, s32[2048]{0:T(1024)S(1)}, /*index=5*/bf16[2...) while((s32[]{:T(128)}, f32[4,512,128]{2,1,0:T(8,128)S(1)}, ...), condition=%wide.region_2.3_spmd, body=%wide.region_0.2_spmd.sunk | while | flops 274726912 | bytes 823421 | solution.py:35
  24.1 0.6 dynamic_slice.9
  24.8 0.6 iota_add_fusion.4
  25.4 0.5 convert_reduce_fusion.4
  26.0 0.8 fusion.198
  26.8 0.6 dynamic_slice.9
  27.4 0.6 iota_add_fusion.4
  28.0 0.5 convert_reduce_fusion.4
  28.6 0.8 fusion.198
  29.4 0.6 dynamic_slice.9
  30.0 0.6 iota_add_fusion.4
  30.7 0.5 convert_reduce_fusion.4
  31.3 0.8 fusion.198
  32.1 0.6 dynamic_slice.9
  32.7 0.6 iota_add_fusion.4
  33.3 0.5 convert_reduce_fusion.4
  33.9 0.8 fusion.198
  34.7 4.4 %all-to-all-done = bf16[8,272,128]{2,1,0:T(8,128)(2,1)S(1)} async-done(((bf16[8,272,128]{2,1,0:T(8,128)(2,1)}), bf16[8,272,128]{2,1,0:T(8,128)(2,1)S(1)}, u32[]{:S(2)}, u32[]{:S(2)}) %all-to-all-start) | async-done | bytes 557088 | tf_op jit(solution)/shard_map/all_to_all | solution.py:91
  39.4 10.6 %while.25 = (s32[]{:T(128)}, f32[4,512,128]{2,1,0:T(8,128)S(1)}, f32[4,512]{1,0:T(4,128)S(1)}, s32[4]{0:T(128)S(1)}, s32[2048]{0:T(1024)S(1)}, /*index=5*/bf16[2...) while((s32[]{:T(128)}, f32[4,512,128]{2,1,0:T(8,128)S(1)}, ...), condition=%wide.region_6.7_spmd, body=%wide.region_4.6_spmd.sunk | while | flops 274726912 | bytes 823421 | solution.py:35
  39.4 0.6 dynamic_slice.10
  40.0 0.6 iota_add_fusion.5
  40.7 0.5 convert_reduce_fusion.5
  41.3 0.8 fusion.200
  42.0 0.6 dynamic_slice.10
  42.7 0.6 iota_add_fusion.5
  43.9 0.8 fusion.200
  44.7 0.6 dynamic_slice.10
  45.3 0.6 iota_add_fusion.5
  46.6 0.8 fusion.200
  47.4 0.6 dynamic_slice.10
  48.0 0.6 iota_add_fusion.5
  49.2 0.8 fusion.200
  50.9 3.6 %collective-permute-start = (bf16[3,256,128]{2,1,0:T(8,128)(2,1)S(1)}, bf16[3,256,128]{2,1,0:T(8,128)(2,1)S(1)}, u32[]{:S(2)}, u32[]{:S(2)}) collective-permute-start(bf16[3,256,128]{2,1,0:T(8,128)(2,1)S(1)} %bitcast.156), channel_id=1, source_target_pairs={{0,1},{1,2},{2,3},{3,4},{4,5},{5,6},{6,7},{8,9},{9,10},{10,11},{11... | collective-permute-start | bytes 589832 | tf_op jit(solution)/shard_map/ppermute | solution.py:14
  54.5 0.7 add_convert_fusion
  55.2 2.5 %collective-permute-done = bf16[3,256,128]{2,1,0:T(8,128)(2,1)S(1)} collective-permute-done((bf16[3,256,128]{2,1,0:T(8,128)(2,1)S(1)}, bf16[3,256,128]{2,1,0:T(8,128)(2,1)S(1)}, u32[]{:S(2)}, u32[]{:S(2)}) %collective-permute-start) | collective-permute-done | bytes 196640 | tf_op jit(solution)/shard_map/ppermute | solution.py:14
  58.2 3.2 %fusion.169 = (bf16[5,1,128,1,128]{4,3,2,1,0:T(2,128)(2,1)S(1)}, bf16[5,1,128,1,128]{4,3,2,1,0:T(2,128)(2,1)S(1)}, bf16[5,1,128,1,128]{4,3,2,1,0:T(2,128)(2,1)S(...) fusion(bf16[6,2,129,2,128]{4,3,2,1,0:T(2,128)(2,1)S(1)} %reshap, ...), kind=kLoop, calls=%fused_computation.236 | loop fusion | bytes 2949120 | tf_op jit(solution)/shard_map/slice | solution.py:48
  61.7 0.7 copy-done.3
  63.9 0.9 fusion.37
  67.1 0.6 convolution_convert_fusion
  67.8 0.8 copy-done.1
  68.6 73.9 %all-gather.2.cloned.1.call-done = bf16[8,8,2,64,256]{4,3,2,1,0:T(8,128)(2,1)} async-done(((bf16[1,8,2,64,256]{4,3,2,1,0:T(8,128)(2,1)}), bf16[8,8,2,64,256]{4,3,2,1,0:T(8,128)(2,1)}) %all-gather.2.cloned.1.call-update) | async-done | bytes 4194320 | tf_op jit(solution)/shard_map/all_gather | solution.py:135
  142.5 3.8 %reduce_sum.40 = bf16[8,2,64,256]{3,2,1,0:T(8,128)(2,1)} reduce(bf16[8,8,2,64,256]{4,3,2,1,0:T(8,128)(2,1)} %all-gather.2.cloned.1.call-done, bf16[]{:T(256)} %constant.62.clone.1), dimensions={0}, to_apply=%region_7.8 | reduce | flops 1835008 | bytes 4718594 | tf_op jit(solution)/shard_map/reduce_sum | solution.py:135
  (109 shorter events, 7.8 us)
Async XLA Ops:
  6.5 6.0 %copy-start = (bf16[2048,128]{1,0:T(8,128)(2,1)S(1)}, bf16[2048,128]{1,0:T(8,128)(2,1)}, u32[]{:S(2)}) copy-start(bf16[2048,128]{1,0:T(8,128)(2,1)} %param.17) | copy-start | bytes 1572868
  7.3 2.2 %copy-start.5 = (s32[2048,1]{0,1:T(1,128)S(1)}, s32[2048,1]{0,1:T(1,128)}, u32[]{:S(2)}) copy-start(s32[2048,1]{0,1:T(1,128)} %param.18) | copy-start | bytes 24580
  7.3 2.3 %copy-start.7 = (s32[2048]{0:T(1024)S(1)}, s32[2048]{0:T(1024)}, u32[]{:S(2)}) copy-start(s32[2048]{0:T(1024)} %param.19) | copy-start | bytes 24580
  15.6 8.5 %copy-start.6 = (s32[2048]{0:T(1024)S(1)}, s32[2048]{0:T(1024)}, u32[]{:S(2)}) copy-start(s32[2048]{0:T(1024)} %param.23) | copy-start | bytes 24580
  15.6 8.6 %copy-start.4 = (s32[2048]{0:T(1024)S(1)}, s32[2048]{0:T(1024)}, u32[]{:S(2)}) copy-start(s32[2048]{0:T(1024)} %param.22) | copy-start | bytes 24580
  15.6 8.6 %copy-start.9 = (bf16[2048,128]{1,0:T(8,128)(2,1)S(1)}, bf16[2048,128]{1,0:T(8,128)(2,1)}, u32[]{:S(2)}) copy-start(bf16[2048,128]{1,0:T(8,128)(2,1)} %param.21) | copy-start | bytes 1572868
  16.7 22.5 %all-to-all-start = ((bf16[8,272,128]{2,1,0:T(8,128)(2,1)}), bf16[8,272,128]{2,1,0:T(8,128)(2,1)S(1)}, u32[]{:S(2)}, u32[]{:S(2)}) async-start(bf16[8,272,128]{2,1,0:T(8,128)(2,1)} %maximum_maximum_fusion), calls=%async_computation | async-start | bytes 1114112 | tf_op jit(solution)/shard_map/all_to_all | solution.py:91
  23.9 118.6 %all-gather.2.cloned.1.call-start = ((), (), s32[]{:S(2)}) async-start(), calls=%async_computation.1 | async-start | bytes 4718592 | tf_op jit(solution)/shard_map/all_gather | solution.py:135
  50.0 0.7 copy-start.8
  50.9 6.8 %collective-permute-start = (bf16[3,256,128]{2,1,0:T(8,128)(2,1)S(1)}, bf16[3,256,128]{2,1,0:T(8,128)(2,1)S(1)}, u32[]{:S(2)}, u32[]{:S(2)}) collective-permute-start(bf16[3,256,128]{2,1,0:T(8,128)(2,1)S(1)} %bitcast.156), channel_id=1, source_target_pairs={{0,1},{1,2},{2,3},{3,4},{4,5},{5,6},{6,7},{8,9},{9,10},{10,11},{11... | collective-permute-start | bytes 589832 | tf_op jit(solution)/shard_map/ppermute | solution.py:14
  61.5 1.0 copy-start.3
  63.0 0.9 copy-start.12
  64.8 1.1 copy-start.2
  65.6 1.5 copy-start.10
  65.6 1.5 copy-start.11
  67.7 0.8 copy-start.1
Sparse Core Ops, SparseCore 0:
  68.7 73.7 all-gather.1
